TPU v7x, 128 devices: a whole 4x4x4 slice. The times are simulated.
128 devices in a mesh: req: 8 (over y, core), voc: 16 (over x, z).
Axes of the slice: x: 4, y: 4, z: 4, core: 2. Of those that a mesh axis runs over, the one named last changes fastest.
Arguments:
- hidden: bfloat16 [16384, 1536], P(('req', 'voc')), may hold values from -64 to 64
- norm_gain: float32 [1536], replicated, may hold values from 0.1 to 1.9
- head: bfloat16 [1536, 49152], P(None, 'voc'), may hold values from -8 to 8
- targets: int32 [16384], P(('req', 'voc')), may hold values from 0 to 49151
- bounds: int32 [128, 2], P(('req', 'voc')), may hold values from 0 to 128, as said below
Outputs:
- logprob: float32 [16384], P(('req', 'voc'))
- entropy: float32 [16384], P(('req', 'voc'))
- target_logit: float32 [16384], P(('req', 'voc'))
- mean_entropy: float32 [1], replicated
Inputs may be any that keep to these rules, and one draw needn't show every extreme that they name: bounds[d] = (lo, hi): slots lo to hi - 1 of device d hold live response rows; 1 <= hi - lo <= 96, lo <= 32; some device has hi - lo = 96 and hi = 128, some has lo = 0.
All inputs are finite; a program needn't handle non-finite values.
Results may differ from a plain program's by a relative error of at most 0.00075.
The roundings to bfloat16 on the way count: a program that leaves them out, or rounds other values in their place, can miss the bound.
Values may be sent and summed in bfloat16 or wider, within the bound.
No kernel may reach another device: no remote copies, remote signals or barrier semaphores. Data moves between devices by JAX's collectives and lax.ppermute only.
A program may use at most 64 MiB of HBM per device.

v0:
```python
import jax
import jax.numpy as jnp
from jax import lax
from jax.sharding import PartitionSpec as P


def joined(part, axis, combine):
    gathered = jax.tree.map(lambda a: lax.all_gather(a, axis), part)

    def take(source):
        return jax.tree.map(lambda a: lax.dynamic_index_in_dim(a, source, 0, False), gathered)

    return lax.fori_loop(
        1, lax.axis_size(axis), lambda source, state: combine(state, take(source)), take(0)
    )


def pick_block(count):
    size = min(count, 512)
    while count % size:
        size -= 1
    return size


def combine_stats(first, second):
    top = jnp.maximum(first[0], second[0])
    weight_a = jnp.exp(first[0] - top)
    weight_b = jnp.exp(second[0] - top)
    return (
        top,
        first[1] * weight_a + second[1] * weight_b,
        first[2] * weight_a + second[2] * weight_b,
        first[3] + second[3],
    )


def shard_stats(gathered, local_ids, head):
    count = gathered.shape[0]
    width = gathered.shape[1]
    block = pick_block(count)
    columns = jnp.arange(head.shape[1], dtype=jnp.int32)

    def one_block(pair):
        rows_in, ids = pair
        logits = jnp.dot(rows_in, head, preferred_element_type=jnp.float32)
        top = jnp.max(logits, axis=-1)
        expo = jnp.exp(logits - top[:, None])
        total = jnp.sum(expo, axis=-1)
        weighted = jnp.sum(expo * logits, axis=-1)
        picked = jnp.sum(jnp.where(columns[None, :] == ids[:, None], logits, 0.0), axis=-1)
        return (top, total, weighted, picked)

    outputs = lax.map(
        one_block,
        (gathered.reshape(count // block, block, width), local_ids.reshape(count // block, block)),
    )
    return tuple((a.reshape(count) for a in outputs))


def shards(hidden, norm_gain, head, targets, bounds):
    slots = hidden.shape[0]
    shard_width = head.shape[1]
    position = lax.axis_index("voc")
    values = hidden.astype(jnp.float32)
    meansq = jnp.mean(values * values, axis=-1, keepdims=True)
    normed = (values * lax.rsqrt(meansq + 1e-05) * norm_gain).astype(jnp.bfloat16)
    start = bounds[0, 0]
    finish = bounds[0, 1]
    gathered, gathered_ids = (
        lax.all_gather(normed, "voc", axis=0, tiled=True),
        lax.all_gather(targets, "voc", axis=0, tiled=True),
    )
    local_ids = gathered_ids - position * shard_width
    stats = shard_stats(gathered, local_ids, head)
    merged = joined(stats, "voc", combine_stats)
    top, total, weighted, picked = [
        lax.dynamic_slice_in_dim(a, position * slots, slots, 0) for a in merged
    ]
    lse = top + jnp.log(total)
    row_entropy = lse - weighted / total
    row_logprob = picked - lse
    slot_index = jnp.arange(slots, dtype=jnp.int32)
    live = (slot_index >= start) & (slot_index < finish)
    zero = jnp.zeros((slots,), jnp.float32)
    entropy = jnp.where(live, row_entropy, zero)
    logprob = jnp.where(live, row_logprob, zero)
    target_logit = jnp.where(live, picked, zero)
    ent_sum, live_count = lax.psum(
        (jnp.sum(entropy), jnp.sum(live.astype(jnp.float32))), ("req", "voc")
    )
    mean_entropy = (ent_sum / live_count).reshape(1)
    return (logprob, entropy, target_logit, mean_entropy)


def solution(mesh):
    placed = (
        P(("req", "voc"), None),
        P(),
        P(None, "voc"),
        P(("req", "voc")),
        P(("req", "voc"), None),
    )
    return jax.shard_map(
        shards,
        mesh=mesh,
        in_specs=placed,
        out_specs=(P(("req", "voc")), P(("req", "voc")), P(("req", "voc")), P()),
        check_vma=False,
    )
```

profile of v0, /device:TPU:1, one launch (start us, length us, event | category | flops | bytes accessed | tf_op | source)
XLA Modules:
  0.0 286.2 jit_solution(3310339040187960190)
XLA Ops:
  7.2 0.0 all-gather.7.cloned.1.call-start
  7.2 1.2 fusion.7
  8.4 1.9 fusion.9
  10.3 0.0 all-gather.7.cloned.1.call-update
  10.4 18.7 %all-gather = s32[16,1,128]{2,1,0:T(1,128)S(1)} all-gather(s32[1,1,128]{2,1,0:T(1,128)} %bitcast.76), channel_id=1, replica_groups=mesh['req'=8,'voc'=16] {'voc'}, dimensions={0}, use_global_device_ids=true | all-gather | bytes 8704 | tf_op jit(solution)/shard_map/all_gather | solution.py:71
  29.1 1.3 fusion.12
  30.5 2.0 convert_reduce_fusion
  32.4 42.5 %all-gather.7.cloned.1.call-done = bf16[2048,1536]{1,0:T(8,128)(2,1)} async-done(((bf16[128,1536]{1,0:T(8,128)(2,1)}), bf16[2048,1536]{1,0:T(8,128)(2,1)}) %all-gather.7.cloned.1.call-update) | async-done | bytes 6291472 | tf_op jit(solution)/shard_map/all_gather | solution.py:70
  74.9 44.3 %while.39 = (s32[]{:T(128)}, f32[4,512]{1,0:T(4,128)S(1)}, f32[4,512]{1,0:T(4,128)S(1)}, f32[4,512]{1,0:T(4,128)S(1)}, f32[4,512]{1,0:T(4,128)S(1)}, /*index=5*/...) while((s32[]{:T(128)}, f32[4,512]{1,0:T(4,128)S(1)}, ...), condition=%wide.region_6.7_spmd.clone, body=%wide.region_1.6_spmd.clone.sunk | while | flops 4844419072 | bytes 23626360 | solution.py:53
  74.9 8.2 %fusion.17 = (f32[512]{0:T(512)S(1)}, f32[512,3072]{1,0:T(8,128)S(1)}) fusion(bf16[1536,3072]{1,0:T(8,128)(2,1)} %get-tuple-element.510, bf16[4,512,1536]{2,1,0:T(8,128)(2,1)} %get-tuple-element.509, s32[]{:T(128)} %get-tuple-element.494), kind=kOutput, calls=%fused_computation.37.clone.1 | convolution fusion | flops 4833410560 | bytes 17304064 | tf_op jit(solution)/shard_map/while/body/eval_jaxpr/dot_general | solution.py:45
  83.2 2.6 multiply_reduce_fusion.2
  85.8 0.1 dynamic_update_slice.24
  85.9 0.1 dynamic_update_slice.22
  85.9 0.1 dynamic_update_slice.21
  86.0 8.2 %fusion.17 = (f32[512]{0:T(512)S(1)}, f32[512,3072]{1,0:T(8,128)S(1)}) fusion(bf16[1536,3072]{1,0:T(8,128)(2,1)} %get-tuple-element.510, bf16[4,512,1536]{2,1,0:T(8,128)(2,1)} %get-tuple-element.509, s32[]{:T(128)} %get-tuple-element.494), kind=kOutput, calls=%fused_computation.37.clone.1 | convolution fusion | flops 4833410560 | bytes 17304064 | tf_op jit(solution)/shard_map/while/body/eval_jaxpr/dot_general | solution.py:45
  94.3 2.6 multiply_reduce_fusion.2
  96.9 0.1 dynamic_update_slice.24
  97.0 0.1 dynamic_update_slice.22
  97.0 0.1 dynamic_update_slice.21
  97.1 8.2 %fusion.17 = (f32[512]{0:T(512)S(1)}, f32[512,3072]{1,0:T(8,128)S(1)}) fusion(bf16[1536,3072]{1,0:T(8,128)(2,1)} %get-tuple-element.510, bf16[4,512,1536]{2,1,0:T(8,128)(2,1)} %get-tuple-element.509, s32[]{:T(128)} %get-tuple-element.494), kind=kOutput, calls=%fused_computation.37.clone.1 | convolution fusion | flops 4833410560 | bytes 17304064 | tf_op jit(solution)/shard_map/while/body/eval_jaxpr/dot_general | solution.py:45
  105.4 2.6 multiply_reduce_fusion.2
  108.0 0.1 dynamic_update_slice.24
  108.1 0.1 dynamic_update_slice.22
  108.1 0.1 dynamic_update_slice.21
  108.2 8.2 %fusion.17 = (f32[512]{0:T(512)S(1)}, f32[512,3072]{1,0:T(8,128)S(1)}) fusion(bf16[1536,3072]{1,0:T(8,128)(2,1)} %get-tuple-element.510, bf16[4,512,1536]{2,1,0:T(8,128)(2,1)} %get-tuple-element.509, s32[]{:T(128)} %get-tuple-element.494), kind=kOutput, calls=%fused_computation.37.clone.1 | convolution fusion | flops 4833410560 | bytes 17304064 | tf_op jit(solution)/shard_map/while/body/eval_jaxpr/dot_general | solution.py:45
  116.5 2.6 multiply_reduce_fusion.2
  119.1 0.1 dynamic_update_slice.24
  119.2 0.1 dynamic_update_slice.22
  119.2 0.1 dynamic_update_slice.21
  119.3 18.0 %all-gather.3 = f32[16,1,2048]{2,1,0:T(1,128)S(1)} all-gather(f32[1,1,2048]{2,1,0:T(1,128)S(1)} %reshape.39), channel_id=1, replica_groups=mesh['req'=8,'voc'=16] {'voc'}, dimensions={0}, use_global_device_ids=true | all-gather | bytes 139264 | tf_op jit(solution)/shard_map/all_gather | solution.py:8
  137.4 16.5 %all-gather.4 = f32[16,1,2048]{2,1,0:T(1,128)S(1)} all-gather(f32[1,1,2048]{2,1,0:T(1,128)S(1)} %reshape.41), channel_id=1, replica_groups=mesh['req'=8,'voc'=16] {'voc'}, dimensions={0}, use_global_device_ids=true | all-gather | bytes 139264 | tf_op jit(solution)/shard_map/all_gather | solution.py:8
  154.0 17.0 %all-gather.1 = f32[16,1,2048]{2,1,0:T(1,128)S(1)} all-gather(f32[1,1,2048]{2,1,0:T(1,128)S(1)} %reshape.35), channel_id=1, replica_groups=mesh['req'=8,'voc'=16] {'voc'}, dimensions={0}, use_global_device_ids=true | all-gather | bytes 139264 | tf_op jit(solution)/shard_map/all_gather | solution.py:8
  171.2 16.8 %all-gather.2 = f32[16,1,2048]{2,1,0:T(1,128)S(1)} all-gather(f32[1,1,2048]{2,1,0:T(1,128)S(1)} %reshape.37), channel_id=1, replica_groups=mesh['req'=8,'voc'=16] {'voc'}, dimensions={0}, use_global_device_ids=true | all-gather | bytes 139264 | tf_op jit(solution)/shard_map/all_gather | solution.py:8
  188.0 2.1 while.38
  190.1 1.2 fusion.10
  191.3 85.5 %all-reduce = (f32[]{:T(128)}, f32[]{:T(128)}) all-reduce(f32[]{:T(128)} %get-tuple-element.346, f32[]{:T(128)} %get-tuple-element.344), channel_id=1, replica_groups=mesh['req'=8,'voc'=16] {'req','voc'}, use_global_device_ids=true, to_apply=%region_10.11 | all-reduce | flops 2 | bytes 16 | tf_op jit(solution)/shard_map/psum | solution.py:88
  (117 shorter events, 1.7 us)
Async XLA Ops:
  7.2 67.8 %all-gather.7.cloned.1.call-start = ((), (), s32[]{:S(2)}) async-start(), calls=%async_computation | async-start | bytes 6684672 | tf_op jit(solution)/shard_map/all_gather | solution.py:70
Sparse Core Ops, SparseCore 0:
  10.5 64.4 all-gather.6
where the time goes:
time: 287 us; the launch traced here: 286 us
  blocking collectives  173 us (60%)
  waiting for transfers between devices  42.5 us (15%)
  matrix products  32.9 us (11%)
  other arithmetic  17.2 us (6%)
  between operations  16.7 us (6%)
  local copies, waits for them, and re-layouts  3.1 us (1%)
    psum x1, blocking collectives, shards(): lax.psum((jnp.sum(entropy), jnp.sum(live.astype(jnp.float32))), ('req', '...  85.5 us
    all_gather x4, blocking collectives, joined(): gathered = jax.tree.map(lambda a: lax.all_gather(a, axis), part)  68.4 us
    all_gather x1, waiting for transfers between devices, shards(): lax.all_gather(normed, 'voc', axis=0, tiled=True)  42.5 us
    dot_general x4, matrix products, one_block(): logits = jnp.dot(rows_in, head, preferred_element_type=jnp.float32)  32.9 us
    all_gather x1, blocking collectives, shards(): lax.all_gather(targets, 'voc', axis=0, tiled=True)  18.7 us
    reduce_sum x4, other arithmetic, one_block(): weighted = jnp.sum(expo * logits, axis=-1)  10.4 us
  transfers between devices with their start and end apart: 1, of which 1 were waited for; matrix products, arithmetic and copies ran while one was open for 1% of the time, Pallas kernels for 0%

commit v1 on v0

--- a/solution.py
+++ b/solution.py
@@ -2,6 +2,22 @@
 import jax.numpy as jnp
 from jax import lax
 from jax.sharding import PartitionSpec as P
+
+
+def collect(x, axis, dim):
+    ways, here, step = (lax.axis_size(axis), lax.axis_index(axis), x.shape[dim])
+    shape = [n * ways if d == dim else n for d, n in enumerate(x.shape)]
+    full = lax.dynamic_update_slice_in_dim(jnp.zeros(shape, x.dtype), x, here * step, axis=dim)
+    going_up = going_down = x
+    for far in range(1, ways // 2 + 1):
+        going_up = lax.ppermute(going_up, axis, [(d, (d + 1) % ways) for d in range(ways)])
+        full = lax.dynamic_update_slice_in_dim(full, going_up, (here - far) % ways * step, axis=dim)
+        if 2 * far < ways:
+            going_down = lax.ppermute(going_down, axis, [(d, (d - 1) % ways) for d in range(ways)])
+            full = lax.dynamic_update_slice_in_dim(
+                full, going_down, (here + far) % ways * step, axis=dim
+            )
+    return full
 
 
 def joined(part, axis, combine):
@@ -67,7 +83,7 @@
     start = bounds[0, 0]
     finish = bounds[0, 1]
     gathered, gathered_ids = (
-        lax.all_gather(normed, "voc", axis=0, tiled=True),
+        collect(normed, "voc", 0),
         lax.all_gather(targets, "voc", axis=0, tiled=True),
     )
     local_ids = gathered_ids - position * shard_width

time: 287 us -> 330 us (1.15)
  starting transfers between devices: 0.04 us -> 36.7 us
  local copies, waits for them, and re-layouts: 3.1 us -> 17.2 us
  between operations: 16.7 us -> 3.31 us
  blocking collectives: 173 us -> 182 us
    all_gather x1 -> x0, waiting for transfers between devices: 42.5 us -> none  [shards(): lax.all_gather(normed, 'voc', axis=0, tiled=True)]
    ppermute x0 -> x15, waiting for transfers between devices: none -> 40.1 us  [the longest x8 39.5 us: collect(): lax.ppermute(going_up, axis, [(d, (d + 1) % ways) for d in range(ways)])]
    ppermute x0 -> x15, starting transfers between devices: none -> 36.7 us  [the longest x7 34.2 us: collect(): lax.ppermute(going_down, axis, [(d, (d - 1) % ways) for d in range(ways)])]
    dynamic_update_slice x0 -> x15, local copies, waits for them, and re-layouts: none -> 11.8 us  [the longest x8 6.25 us: collect(): lax.dynamic_update_slice_in_dim(full, going_up, (here - far) % ways * ste...]
    psum x1, blocking collectives: 85.5 us -> 96.4 us  [shards(): lax.psum((jnp.sum(entropy), jnp.sum(live.astype(jnp.float32))), ('req', '...]
  transfers between devices with their start and end apart: 1 -> 15, of which waited for: 1 -> 9; matrix products, arithmetic and copies ran while one was open for 1% -> 4% of each run, Pallas kernels for 0% -> 0%
where the time goes in v1:
time: 330 us
  blocking collectives  182 us (55%)
  waiting for transfers between devices  40.1 us (12%)
  starting transfers between devices  36.7 us (11%)
  matrix products  32.9 us (10%)
  local copies, waits for them, and re-layouts  17.2 us (5%)
  other arithmetic  16.1 us (5%)
  between operations  3.31 us (1%)
    psum x1, blocking collectives, shards(): lax.psum((jnp.sum(entropy), jnp.sum(live.astype(jnp.float32))), ('req', '...  96.4 us
    all_gather x4, blocking collectives, joined(): gathered = jax.tree.map(lambda a: lax.all_gather(a, axis), part)  67.2 us
    ppermute x8, waiting for transfers between devices, collect(): lax.ppermute(going_up, axis, [(d, (d + 1) % ways) for d in range(ways)])  39.5 us
    ppermute x7, starting transfers between devices, collect(): lax.ppermute(going_down, axis, [(d, (d - 1) % ways) for d in range(ways)])  34.2 us
    dot_general x4, matrix products, one_block(): logits = jnp.dot(rows_in, head, preferred_element_type=jnp.float32)  32.9 us
    all_gather x1, blocking collectives, shards(): lax.all_gather(targets, 'voc', axis=0, tiled=True)  18.9 us
    reduce_sum x4, other arithmetic, one_block(): weighted = jnp.sum(expo * logits, axis=-1)  10.4 us
  transfers between devices with their start and end apart: 15, of which 9 were waited for; matrix products, arithmetic and copies ran while one was open for 4% of the time, Pallas kernels for 0%

profile of v1, /device:TPU:1, one launch (start us, length us, event | category | flops | bytes accessed | tf_op | source)
XLA Modules:
  0.0 329.8 jit_solution(3257770971862297256)
XLA Ops:
  0.7 1.2 fusion.7
  1.9 3.1 broadcast_in_dim.28
  5.0 0.9 constant_dynamic-update-slice_fusion.15
  5.9 2.5 collective-permute-start
  8.3 4.3 %collective-permute-start.1 = (bf16[128,1536]{1,0:T(8,128)(2,1)S(1)}, bf16[128,1536]{1,0:T(8,128)(2,1)S(1)}, u32[]{:S(2)}, u32[]{:S(2)}) collective-permute-start(bf16[128,1536]{1,0:T(8,128)(2,1)S(1)} %get-tuple-element.349), channel_id=1, source_target_pairs={{0,15},{1,0},{2,1},{3,2},{4,3},{5,4},{6,5},{7,6},{8,7},{9,8},{10,9... | collective-permute-start | bytes 1179656 | tf_op jit(solution)/shard_map/ppermute | solution.py:16
  12.6 18.9 %all-gather = s32[16,1,128]{2,1,0:T(1,128)S(1)} all-gather(s32[1,1,128]{2,1,0:T(1,128)S(1)} %bitcast.76), channel_id=1, replica_groups=mesh['req'=8,'voc'=16] {'voc'}, dimensions={0}, use_global_device_ids=true | all-gather | bytes 8704 | tf_op jit(solution)/shard_map/all_gather | solution.py:87
  32.3 2.0 convert_reduce_fusion
  34.2 4.8 %collective-permute-start.3 = (bf16[128,1536]{1,0:T(8,128)(2,1)S(1)}, bf16[128,1536]{1,0:T(8,128)(2,1)S(1)}, u32[]{:S(2)}, u32[]{:S(2)}) collective-permute-start(bf16[128,1536]{1,0:T(8,128)(2,1)S(1)} %collective-permute-done.1), channel_id=1, source_target_pairs={{0,15},{1,0},{2,1},{3,2},{4,3},{5,4},{6,5},{7,6},{8,7},{9,8},{10,9... | collective-permute-start | bytes 1179656 | tf_op jit(solution)/shard_map/ppermute | solution.py:16
  39.8 0.8 constant_dynamic-update-slice_fusion.13
  40.6 3.6 %collective-permute-done.2 = bf16[128,1536]{1,0:T(8,128)(2,1)S(1)} collective-permute-done((bf16[128,1536]{1,0:T(8,128)(2,1)S(1)}, bf16[128,1536]{1,0:T(8,128)(2,1)S(1)}, u32[]{:S(2)}, u32[]{:S(2)}) %collective-permute-start.2) | collective-permute-done | bytes 393248 | tf_op jit(solution)/shard_map/ppermute | solution.py:13
  44.2 4.8 %collective-permute-start.5 = (bf16[128,1536]{1,0:T(8,128)(2,1)S(1)}, bf16[128,1536]{1,0:T(8,128)(2,1)S(1)}, u32[]{:S(2)}, u32[]{:S(2)}) collective-permute-start(bf16[128,1536]{1,0:T(8,128)(2,1)S(1)} %collective-permute-done.3), channel_id=1, source_target_pairs={{0,15},{1,0},{2,1},{3,2},{4,3},{5,4},{6,5},{7,6},{8,7},{9,8},{10,9... | collective-permute-start | bytes 1179656 | tf_op jit(solution)/shard_map/ppermute | solution.py:16
  49.0 0.8 constant_dynamic-update-slice_fusion.12
  49.8 0.8 constant_dynamic-update-slice_fusion.11
  50.6 3.6 %collective-permute-done.4 = bf16[128,1536]{1,0:T(8,128)(2,1)S(1)} collective-permute-done((bf16[128,1536]{1,0:T(8,128)(2,1)S(1)}, bf16[128,1536]{1,0:T(8,128)(2,1)S(1)}, u32[]{:S(2)}, u32[]{:S(2)}) %collective-permute-start.4) | collective-permute-done | bytes 393248 | tf_op jit(solution)/shard_map/ppermute | solution.py:13
  54.1 4.8 %collective-permute-start.7 = (bf16[128,1536]{1,0:T(8,128)(2,1)S(1)}, bf16[128,1536]{1,0:T(8,128)(2,1)S(1)}, u32[]{:S(2)}, u32[]{:S(2)}) collective-permute-start(bf16[128,1536]{1,0:T(8,128)(2,1)S(1)} %collective-permute-done.5), channel_id=1, source_target_pairs={{0,15},{1,0},{2,1},{3,2},{4,3},{5,4},{6,5},{7,6},{8,7},{9,8},{10,9... | collective-permute-start | bytes 1179656 | tf_op jit(solution)/shard_map/ppermute | solution.py:16
  58.9 0.8 constant_dynamic-update-slice_fusion.10
  59.7 0.8 constant_dynamic-update-slice_fusion.9
  60.5 3.7 %collective-permute-done.6 = bf16[128,1536]{1,0:T(8,128)(2,1)S(1)} collective-permute-done((bf16[128,1536]{1,0:T(8,128)(2,1)S(1)}, bf16[128,1536]{1,0:T(8,128)(2,1)S(1)}, u32[]{:S(2)}, u32[]{:S(2)}) %collective-permute-start.6) | collective-permute-done | bytes 393248 | tf_op jit(solution)/shard_map/ppermute | solution.py:13
  64.2 5.1 %collective-permute-start.9 = (bf16[128,1536]{1,0:T(8,128)(2,1)S(1)}, bf16[128,1536]{1,0:T(8,128)(2,1)S(1)}, u32[]{:S(2)}, u32[]{:S(2)}) collective-permute-start(bf16[128,1536]{1,0:T(8,128)(2,1)S(1)} %collective-permute-done.7), channel_id=1, source_target_pairs={{0,15},{1,0},{2,1},{3,2},{4,3},{5,4},{6,5},{7,6},{8,7},{9,8},{10,9... | collective-permute-start | bytes 1179656 | tf_op jit(solution)/shard_map/ppermute | solution.py:16
  69.2 0.8 constant_dynamic-update-slice_fusion.8
  70.0 0.8 constant_dynamic-update-slice_fusion.7
  70.8 4.6 %collective-permute-done.8 = bf16[128,1536]{1,0:T(8,128)(2,1)S(1)} collective-permute-done((bf16[128,1536]{1,0:T(8,128)(2,1)S(1)}, bf16[128,1536]{1,0:T(8,128)(2,1)S(1)}, u32[]{:S(2)}, u32[]{:S(2)}) %collective-permute-start.8) | collective-permute-done | bytes 393248 | tf_op jit(solution)/shard_map/ppermute | solution.py:13
  75.5 5.2 %collective-permute-start.11 = (bf16[128,1536]{1,0:T(8,128)(2,1)S(1)}, bf16[128,1536]{1,0:T(8,128)(2,1)S(1)}, u32[]{:S(2)}, u32[]{:S(2)}) collective-permute-start(bf16[128,1536]{1,0:T(8,128)(2,1)S(1)} %collective-permute-done.9), channel_id=1, source_target_pairs={{0,15},{1,0},{2,1},{3,2},{4,3},{5,4},{6,5},{7,6},{8,7},{9,8},{10,9... | collective-permute-start | bytes 1179656 | tf_op jit(solution)/shard_map/ppermute | solution.py:16
  80.7 0.8 constant_dynamic-update-slice_fusion.6
  81.5 0.8 constant_dynamic-update-slice_fusion.5
  82.3 5.4 %collective-permute-done.10 = bf16[128,1536]{1,0:T(8,128)(2,1)S(1)} collective-permute-done((bf16[128,1536]{1,0:T(8,128)(2,1)S(1)}, bf16[128,1536]{1,0:T(8,128)(2,1)S(1)}, u32[]{:S(2)}, u32[]{:S(2)}) %collective-permute-start.10) | collective-permute-done | bytes 393248 | tf_op jit(solution)/shard_map/ppermute | solution.py:13
  88.1 5.2 %collective-permute-start.13 = (bf16[128,1536]{1,0:T(8,128)(2,1)S(1)}, bf16[128,1536]{1,0:T(8,128)(2,1)S(1)}, u32[]{:S(2)}, u32[]{:S(2)}) collective-permute-start(bf16[128,1536]{1,0:T(8,128)(2,1)S(1)} %collective-permute-done.11), channel_id=1, source_target_pairs={{0,15},{1,0},{2,1},{3,2},{4,3},{5,4},{6,5},{7,6},{8,7},{9,8},{10,9... | collective-permute-start | bytes 1179656 | tf_op jit(solution)/shard_map/ppermute | solution.py:16
  94.1 0.8 constant_dynamic-update-slice_fusion.3
  94.9 6.3 %collective-permute-done.12 = bf16[128,1536]{1,0:T(8,128)(2,1)S(1)} collective-permute-done((bf16[128,1536]{1,0:T(8,128)(2,1)S(1)}, bf16[128,1536]{1,0:T(8,128)(2,1)S(1)}, u32[]{:S(2)}, u32[]{:S(2)}) %collective-permute-start.12) | collective-permute-done | bytes 393248 | tf_op jit(solution)/shard_map/ppermute | solution.py:13
  102.0 0.8 constant_dynamic-update-slice_fusion.1
  102.8 12.4 %collective-permute-done.14 = bf16[128,1536]{1,0:T(8,128)(2,1)S(1)} collective-permute-done((bf16[128,1536]{1,0:T(8,128)(2,1)S(1)}, bf16[128,1536]{1,0:T(8,128)(2,1)S(1)}, u32[]{:S(2)}, u32[]{:S(2)}) %collective-permute-start.14) | collective-permute-done | bytes 393248 | tf_op jit(solution)/shard_map/ppermute | solution.py:13
  115.2 0.8 constant_dynamic-update-slice_fusion
  115.9 44.3 %while.39 = (s32[]{:T(128)}, f32[4,512]{1,0:T(4,128)S(1)}, f32[4,512]{1,0:T(4,128)S(1)}, f32[4,512]{1,0:T(4,128)S(1)}, f32[4,512]{1,0:T(4,128)S(1)}, /*index=5*/...) while((s32[]{:T(128)}, f32[4,512]{1,0:T(4,128)S(1)}, ...), condition=%wide.region_6.7_spmd.clone, body=%wide.region_1.6_spmd.clone.sunk | while | flops 4844419072 | bytes 23626360 | solution.py:69
  115.9 8.2 %fusion.18 = (f32[512]{0:T(512)S(1)}, f32[512,3072]{1,0:T(8,128)S(1)}) fusion(bf16[1536,3072]{1,0:T(8,128)(2,1)} %get-tuple-element.512, bf16[4,512,1536]{2,1,0:T(8,128)(2,1)} %get-tuple-element.511, s32[]{:T(128)} %get-tuple-element.496), kind=kOutput, calls=%fused_computation.53.clone.1 | convolution fusion | flops 4833410560 | bytes 17304064 | tf_op jit(solution)/shard_map/while/body/eval_jaxpr/dot_general | solution.py:61
  124.2 2.6 multiply_reduce_fusion.2
  127.0 8.2 %fusion.18 = (f32[512]{0:T(512)S(1)}, f32[512,3072]{1,0:T(8,128)S(1)}) fusion(bf16[1536,3072]{1,0:T(8,128)(2,1)} %get-tuple-element.512, bf16[4,512,1536]{2,1,0:T(8,128)(2,1)} %get-tuple-element.511, s32[]{:T(128)} %get-tuple-element.496), kind=kOutput, calls=%fused_computation.53.clone.1 | convolution fusion | flops 4833410560 | bytes 17304064 | tf_op jit(solution)/shard_map/while/body/eval_jaxpr/dot_general | solution.py:61
  135.3 2.6 multiply_reduce_fusion.2
  138.1 8.2 %fusion.18 = (f32[512]{0:T(512)S(1)}, f32[512,3072]{1,0:T(8,128)S(1)}) fusion(bf16[1536,3072]{1,0:T(8,128)(2,1)} %get-tuple-element.512, bf16[4,512,1536]{2,1,0:T(8,128)(2,1)} %get-tuple-element.511, s32[]{:T(128)} %get-tuple-element.496), kind=kOutput, calls=%fused_computation.53.clone.1 | convolution fusion | flops 4833410560 | bytes 17304064 | tf_op jit(solution)/shard_map/while/body/eval_jaxpr/dot_general | solution.py:61
  146.4 2.6 multiply_reduce_fusion.2
  149.2 8.2 %fusion.18 = (f32[512]{0:T(512)S(1)}, f32[512,3072]{1,0:T(8,128)S(1)}) fusion(bf16[1536,3072]{1,0:T(8,128)(2,1)} %get-tuple-element.512, bf16[4,512,1536]{2,1,0:T(8,128)(2,1)} %get-tuple-element.511, s32[]{:T(128)} %get-tuple-element.496), kind=kOutput, calls=%fused_computation.53.clone.1 | convolution fusion | flops 4833410560 | bytes 17304064 | tf_op jit(solution)/shard_map/while/body/eval_jaxpr/dot_general | solution.py:61
  157.4 2.6 multiply_reduce_fusion.2
  160.3 15.5 %all-gather.3 = f32[16,1,2048]{2,1,0:T(1,128)S(1)} all-gather(f32[1,1,2048]{2,1,0:T(1,128)S(1)} %reshape.39), channel_id=1, replica_groups=mesh['req'=8,'voc'=16] {'voc'}, dimensions={0}, use_global_device_ids=true | all-gather | bytes 139264 | tf_op jit(solution)/shard_map/all_gather | solution.py:24
  175.8 18.1 %all-gather.4 = f32[16,1,2048]{2,1,0:T(1,128)S(1)} all-gather(f32[1,1,2048]{2,1,0:T(1,128)S(1)} %reshape.41), channel_id=1, replica_groups=mesh['req'=8,'voc'=16] {'voc'}, dimensions={0}, use_global_device_ids=true | all-gather | bytes 139264 | tf_op jit(solution)/shard_map/all_gather | solution.py:24
  194.0 16.1 %all-gather.1 = f32[16,1,2048]{2,1,0:T(1,128)S(1)} all-gather(f32[1,1,2048]{2,1,0:T(1,128)S(1)} %reshape.35), channel_id=1, replica_groups=mesh['req'=8,'voc'=16] {'voc'}, dimensions={0}, use_global_device_ids=true | all-gather | bytes 139264 | tf_op jit(solution)/shard_map/all_gather | solution.py:24
  210.2 17.5 %all-gather.2 = f32[16,1,2048]{2,1,0:T(1,128)S(1)} all-gather(f32[1,1,2048]{2,1,0:T(1,128)S(1)} %reshape.37), channel_id=1, replica_groups=mesh['req'=8,'voc'=16] {'voc'}, dimensions={0}, use_global_device_ids=true | all-gather | bytes 139264 | tf_op jit(solution)/shard_map/all_gather | solution.py:24
  227.7 2.1 while.38
  229.8 1.2 fusion.10
  231.1 96.4 %all-reduce = (f32[]{:T(128)}, f32[]{:T(128)}) all-reduce(f32[]{:T(128)} %get-tuple-element.346, f32[]{:T(128)} %get-tuple-element.344), channel_id=1, replica_groups=mesh['req'=8,'voc'=16] {'req','voc'}, use_global_device_ids=true, to_apply=%region_10.11 | all-reduce | flops 2 | bytes 16 | tf_op jit(solution)/shard_map/psum | solution.py:104
  (156 shorter events, 5.7 us)
Async XLA Ops:
  0.6 4.3 %copy-start = (bf16[128,1536]{1,0:T(8,128)(2,1)S(1)}, bf16[128,1536]{1,0:T(8,128)(2,1)}, u32[]{:S(2)}) copy-start(bf16[128,1536]{1,0:T(8,128)(2,1)} %param.9) | copy-start | bytes 1179652
  0.6 4.3 %copy-start.1 = (f32[1536]{0:T(1024)S(1)}, f32[1536]{0:T(1024)}, u32[]{:S(2)}) copy-start(f32[1536]{0:T(1024)} %param.10) | copy-start | bytes 18436
  0.7 12.0 %copy-start.3 = (s32[128]{0:T(128)S(1)}, s32[128]{0:T(128)}, u32[]{:S(2)}) copy-start(s32[128]{0:T(128)} %param.12) | copy-start | bytes 1540
  0.7 31.0 %copy-start.2 = (s32[1,2]{1,0:T(1,128)S(1)}, s32[1,2]{1,0:T(1,128)}, u32[]{:S(2)}) copy-start(s32[1,2]{1,0:T(1,128)} %param.13) | copy-start | bytes 28
  5.9 28.4 %collective-permute-start = (bf16[128,1536]{1,0:T(8,128)(2,1)S(1)}, bf16[128,1536]{1,0:T(8,128)(2,1)S(1)}, u32[]{:S(2)}, u32[]{:S(2)}) collective-permute-start(bf16[128,1536]{1,0:T(8,128)(2,1)S(1)} %get-tuple-element.349), channel_id=1, source_target_pairs={{0,1},{1,2},{2,3},{3,4},{4,5},{5,6},{6,7},{7,8},{8,9},{9,10},{10,1... | collective-permute-start | bytes 1179656 | tf_op jit(solution)/shard_map/ppermute | solution.py:13
  8.3 25.9 %collective-permute-start.1 = (bf16[128,1536]{1,0:T(8,128)(2,1)S(1)}, bf16[128,1536]{1,0:T(8,128)(2,1)S(1)}, u32[]{:S(2)}, u32[]{:S(2)}) collective-permute-start(bf16[128,1536]{1,0:T(8,128)(2,1)S(1)} %get-tuple-element.349), channel_id=1, source_target_pairs={{0,15},{1,0},{2,1},{3,2},{4,3},{5,4},{6,5},{7,6},{8,7},{9,8},{10,9... | collective-permute-start | bytes 1179656 | tf_op jit(solution)/shard_map/ppermute | solution.py:16
  34.2 9.9 %collective-permute-start.2 = (bf16[128,1536]{1,0:T(8,128)(2,1)S(1)}, bf16[128,1536]{1,0:T(8,128)(2,1)S(1)}, u32[]{:S(2)}, u32[]{:S(2)}) collective-permute-start(bf16[128,1536]{1,0:T(8,128)(2,1)S(1)} %collective-permute-done), channel_id=1, source_target_pairs={{0,1},{1,2},{2,3},{3,4},{4,5},{5,6},{6,7},{7,8},{8,9},{9,10},{10,1... | collective-permute-start | bytes 1179656 | tf_op jit(solution)/shard_map/ppermute | solution.py:13
  34.2 9.9 %collective-permute-start.3 = (bf16[128,1536]{1,0:T(8,128)(2,1)S(1)}, bf16[128,1536]{1,0:T(8,128)(2,1)S(1)}, u32[]{:S(2)}, u32[]{:S(2)}) collective-permute-start(bf16[128,1536]{1,0:T(8,128)(2,1)S(1)} %collective-permute-done.1), channel_id=1, source_target_pairs={{0,15},{1,0},{2,1},{3,2},{4,3},{5,4},{6,5},{7,6},{8,7},{9,8},{10,9... | collective-permute-start | bytes 1179656 | tf_op jit(solution)/shard_map/ppermute | solution.py:16
  44.2 9.9 %collective-permute-start.4 = (bf16[128,1536]{1,0:T(8,128)(2,1)S(1)}, bf16[128,1536]{1,0:T(8,128)(2,1)S(1)}, u32[]{:S(2)}, u32[]{:S(2)}) collective-permute-start(bf16[128,1536]{1,0:T(8,128)(2,1)S(1)} %collective-permute-done.2), channel_id=1, source_target_pairs={{0,1},{1,2},{2,3},{3,4},{4,5},{5,6},{6,7},{7,8},{8,9},{9,10},{10,1... | collective-permute-start | bytes 1179656 | tf_op jit(solution)/shard_map/ppermute | solution.py:13
  44.2 9.9 %collective-permute-start.5 = (bf16[128,1536]{1,0:T(8,128)(2,1)S(1)}, bf16[128,1536]{1,0:T(8,128)(2,1)S(1)}, u32[]{:S(2)}, u32[]{:S(2)}) collective-permute-start(bf16[128,1536]{1,0:T(8,128)(2,1)S(1)} %collective-permute-done.3), channel_id=1, source_target_pairs={{0,15},{1,0},{2,1},{3,2},{4,3},{5,4},{6,5},{7,6},{8,7},{9,8},{10,9... | collective-permute-start | bytes 1179656 | tf_op jit(solution)/shard_map/ppermute | solution.py:16
  54.1 10.0 %collective-permute-start.6 = (bf16[128,1536]{1,0:T(8,128)(2,1)S(1)}, bf16[128,1536]{1,0:T(8,128)(2,1)S(1)}, u32[]{:S(2)}, u32[]{:S(2)}) collective-permute-start(bf16[128,1536]{1,0:T(8,128)(2,1)S(1)} %collective-permute-done.4), channel_id=1, source_target_pairs={{0,1},{1,2},{2,3},{3,4},{4,5},{5,6},{6,7},{7,8},{8,9},{9,10},{10,1... | collective-permute-start | bytes 1179656 | tf_op jit(solution)/shard_map/ppermute | solution.py:13
  54.1 10.0 %collective-permute-start.7 = (bf16[128,1536]{1,0:T(8,128)(2,1)S(1)}, bf16[128,1536]{1,0:T(8,128)(2,1)S(1)}, u32[]{:S(2)}, u32[]{:S(2)}) collective-permute-start(bf16[128,1536]{1,0:T(8,128)(2,1)S(1)} %collective-permute-done.5), channel_id=1, source_target_pairs={{0,15},{1,0},{2,1},{3,2},{4,3},{5,4},{6,5},{7,6},{8,7},{9,8},{10,9... | collective-permute-start | bytes 1179656 | tf_op jit(solution)/shard_map/ppermute | solution.py:16
  64.2 11.2 %collective-permute-start.8 = (bf16[128,1536]{1,0:T(8,128)(2,1)S(1)}, bf16[128,1536]{1,0:T(8,128)(2,1)S(1)}, u32[]{:S(2)}, u32[]{:S(2)}) collective-permute-start(bf16[128,1536]{1,0:T(8,128)(2,1)S(1)} %collective-permute-done.6), channel_id=1, source_target_pairs={{0,1},{1,2},{2,3},{3,4},{4,5},{5,6},{6,7},{7,8},{8,9},{9,10},{10,1... | collective-permute-start | bytes 1179656 | tf_op jit(solution)/shard_map/ppermute | solution.py:13
  64.2 11.3 %collective-permute-start.9 = (bf16[128,1536]{1,0:T(8,128)(2,1)S(1)}, bf16[128,1536]{1,0:T(8,128)(2,1)S(1)}, u32[]{:S(2)}, u32[]{:S(2)}) collective-permute-start(bf16[128,1536]{1,0:T(8,128)(2,1)S(1)} %collective-permute-done.7), channel_id=1, source_target_pairs={{0,15},{1,0},{2,1},{3,2},{4,3},{5,4},{6,5},{7,6},{8,7},{9,8},{10,9... | collective-permute-start | bytes 1179656 | tf_op jit(solution)/shard_map/ppermute | solution.py:16
  75.4 12.3 %collective-permute-start.10 = (bf16[128,1536]{1,0:T(8,128)(2,1)S(1)}, bf16[128,1536]{1,0:T(8,128)(2,1)S(1)}, u32[]{:S(2)}, u32[]{:S(2)}) collective-permute-start(bf16[128,1536]{1,0:T(8,128)(2,1)S(1)} %collective-permute-done.8), channel_id=1, source_target_pairs={{0,1},{1,2},{2,3},{3,4},{4,5},{5,6},{6,7},{7,8},{8,9},{9,10},{10,1... | collective-permute-start | bytes 1179656 | tf_op jit(solution)/shard_map/ppermute | solution.py:13
  75.5 12.6 %collective-permute-start.11 = (bf16[128,1536]{1,0:T(8,128)(2,1)S(1)}, bf16[128,1536]{1,0:T(8,128)(2,1)S(1)}, u32[]{:S(2)}, u32[]{:S(2)}) collective-permute-start(bf16[128,1536]{1,0:T(8,128)(2,1)S(1)} %collective-permute-done.9), channel_id=1, source_target_pairs={{0,15},{1,0},{2,1},{3,2},{4,3},{5,4},{6,5},{7,6},{8,7},{9,8},{10,9... | collective-permute-start | bytes 1179656 | tf_op jit(solution)/shard_map/ppermute | solution.py:16
  87.7 13.5 %collective-permute-start.12 = (bf16[128,1536]{1,0:T(8,128)(2,1)S(1)}, bf16[128,1536]{1,0:T(8,128)(2,1)S(1)}, u32[]{:S(2)}, u32[]{:S(2)}) collective-permute-start(bf16[128,1536]{1,0:T(8,128)(2,1)S(1)} %collective-permute-done.10), channel_id=1, source_target_pairs={{0,1},{1,2},{2,3},{3,4},{4,5},{5,6},{6,7},{7,8},{8,9},{9,10},{10,1... | collective-permute-start | bytes 1179656 | tf_op jit(solution)/shard_map/ppermute | solution.py:13
  88.1 13.9 %collective-permute-start.13 = (bf16[128,1536]{1,0:T(8,128)(2,1)S(1)}, bf16[128,1536]{1,0:T(8,128)(2,1)S(1)}, u32[]{:S(2)}, u32[]{:S(2)}) collective-permute-start(bf16[128,1536]{1,0:T(8,128)(2,1)S(1)} %collective-permute-done.11), channel_id=1, source_target_pairs={{0,15},{1,0},{2,1},{3,2},{4,3},{5,4},{6,5},{7,6},{8,7},{9,8},{10,9... | collective-permute-start | bytes 1179656 | tf_op jit(solution)/shard_map/ppermute | solution.py:16
  101.2 14.0 %collective-permute-start.14 = (bf16[128,1536]{1,0:T(8,128)(2,1)S(1)}, bf16[128,1536]{1,0:T(8,128)(2,1)S(1)}, u32[]{:S(2)}, u32[]{:S(2)}) collective-permute-start(bf16[128,1536]{1,0:T(8,128)(2,1)S(1)} %collective-permute-done.12), channel_id=1, source_target_pairs={{0,1},{1,2},{2,3},{3,4},{4,5},{5,6},{6,7},{7,8},{8,9},{9,10},{10,1... | collective-permute-start | bytes 1179656 | tf_op jit(solution)/shard_map/ppermute | solution.py:13
